TPU v7x, 256 devices: a whole 4x4x8 slice. The times are simulated.
256 devices in a mesh: region: 8 (over z), row: 32 (over y, x, core).
Axes of the slice: x: 4, y: 4, z: 8, core: 2. Of those that a mesh axis runs over, the one named last changes fastest.
Arguments:
- state0: float32 [32, 131072], P(None, ('region', 'row')), may hold values from -6 to 6
- drive: bfloat16 [32, 131072], P(None, ('region', 'row')), may hold values from -6 to 6
- cotangent: float32 [32, 131072], P(None, ('region', 'row')), may hold values from -6 to 6
- excitatory: int32 [131072], P(('region', 'row')), may hold values 0 or 1
- tile_vals: bfloat16 [1024, 24, 128, 128], P(('region', 'row')), may hold values from 0.0039978027 to 0.039794922
- tile_cols: int32 [1024, 24], P(('region', 'row')), may hold values from 0 to 159
- tile_count: int32 [1024], P(('region', 'row')), may hold values from 1 to 24, as said below
- boundary_rows: int32 [8, 32, 8, 16], P('region', 'row'), may hold values from 0 to 511, as said below
- u_factor: bfloat16 [32, 131072], P(None, ('region', 'row')), may hold values from -1 to 1
- v_factor: bfloat16 [32, 131072], P(None, ('region', 'row')), may hold values from -0.015625 to 0.015625
Outputs:
- final_state: float32 [32, 131072], P(None, ('region', 'row'))
- grad_u: float32 [32, 131072], P(None, ('region', 'row'))
- grad_v: float32 [32, 131072], P(None, ('region', 'row'))
Inputs may be any that keep to these rules, and one draw needn't show every extreme that they name: tile_count[q] tiles of row tile q are live; its tiles j >= tile_count[q] take no part; the most, 24, is reached in every draw. `boundary_rows`: the 16 rows of one list are distinct. tile_cols[q, j] numbers a tile of 128 extended columns of the group of row tile q.
All inputs are finite; a program needn't handle non-finite values. No bound on the sum of `excitatory` on one device may be relied on, other than what follows from the above.
Results may differ from a plain program's by a relative error of at most 0.0055.
Values may be sent and summed in bfloat16 or wider, within the bound.
No kernel may reach another device: no remote copies, remote signals or barrier semaphores. Data moves between devices by JAX's collectives and lax.ppermute only.
A program may use at most 64 MiB of HBM per device.

v0:
```python
import jax
import jax.numpy as jnp
from jax import lax
from jax.sharding import Mesh
from jax.sharding import PartitionSpec as P

STEPS = 4
ROW = ("row_0", "row_1", "row_2")
REGION_ROW = ("region", "row_0", "row_1", "row_2")
leak = 0.5


def apply_tiles(ext_cols, flat_cols, live_tiles, flat_tiles, row_tiles):
    batch_rows, span_cols = ext_cols.shape
    blocks = ext_cols.reshape(batch_rows, span_cols // 128, 128)[:, flat_cols, :]
    blocks = jnp.where(live_tiles[None, :, None], blocks, jnp.zeros((), blocks.dtype))
    product = jnp.einsum("bsk,sik->bsi", blocks, flat_tiles, preferred_element_type=jnp.float32)
    summed = product.reshape(batch_rows, row_tiles, -1, 128).sum(axis=2)
    return summed.reshape(batch_rows, row_tiles * 128)


def from_each_region(x, me):
    everyone = lax.all_gather(x, "region", axis=0, tiled=False)
    mine = lax.dynamic_index_in_dim(everyone, me, axis=2, keepdims=False)
    return jnp.moveaxis(mine, 0, 1).reshape(x.shape[0], -1)


def local(
    state0,
    drive,
    cotangent,
    excitatory,
    tile_vals,
    tile_cols,
    tile_count,
    boundary_rows,
    u_factor,
    v_factor,
):
    lanes = lax.axis_size(ROW)
    groups = lax.axis_size("region")
    me = lax.axis_index("region")
    own_rows = state0.shape[1]
    own_tiles = own_rows // 128
    row_tiles = tile_vals.shape[0]
    chosen = boundary_rows.reshape(-1)
    bound_cols = chosen.shape[0]
    bound_tiles = bound_cols // 128
    per_lane = own_tiles + bound_tiles
    lane_of = tile_cols // per_lane
    at_lane = tile_cols % per_lane
    remapped = jnp.where(
        at_lane < own_tiles,
        lane_of * own_tiles + at_lane,
        lanes * own_tiles + lane_of * bound_tiles + at_lane - own_tiles,
    )
    flat_cols = remapped.reshape(-1)
    live_grid = jnp.arange(tile_cols.shape[1], dtype=jnp.int32)[None, :] < tile_count[:, None]
    live_tiles = live_grid.reshape(-1)
    flat_tiles = tile_vals.reshape(-1, 128, 128)
    polarity = (2 * excitatory - 1).astype(jnp.float32)
    state = state0
    saved = []
    for moment in range(STEPS):
        rates = jnp.tanh(state)
        signed = (polarity * rates).astype(jnp.bfloat16)
        batch_rows = signed.shape[0]
        gathered_own = lax.all_gather(signed, ROW, axis=1, tiled=True)
        outgoing = jnp.take(signed, chosen, axis=1).reshape(batch_rows, groups, -1)
        incoming = from_each_region(outgoing, me)
        latent = lax.psum(
            jnp.dot(signed, v_factor.T, preferred_element_type=jnp.float32), REGION_ROW
        )
        gathered_border = lax.all_gather(incoming, ROW, axis=1, tiled=True)
        gathered = jnp.concatenate([gathered_own, gathered_border], axis=1)
        synaptic = apply_tiles(gathered, flat_cols, live_tiles, flat_tiles, row_tiles)
        latent_b = latent.astype(jnp.bfloat16)
        lowrank = jnp.dot(latent_b, u_factor, preferred_element_type=jnp.float32)
        saved.append((rates, signed, latent_b))
        state = state + leak * (-state + synaptic + lowrank + drive.astype(jnp.float32))
    grad_u = jnp.zeros((u_factor.shape[0], own_rows), jnp.float32)
    grad_v = jnp.zeros((v_factor.shape[0], own_rows), jnp.float32)
    adjoint = cotangent
    for moment in reversed(range(STEPS)):
        rates, signed, latent_b = saved[moment]
        scaled_b = (leak * adjoint).astype(jnp.bfloat16)
        coeffs = lax.psum(
            jnp.dot(scaled_b, u_factor.T, preferred_element_type=jnp.float32), REGION_ROW
        )
        coeffs_b = coeffs.astype(jnp.bfloat16)
        batch_rows = scaled_b.shape[0]
        spread = jnp.einsum(
            "bri,rjik->brjk",
            scaled_b.reshape(batch_rows, row_tiles, 128),
            tile_vals,
            preferred_element_type=jnp.float32,
        )
        spread = jnp.where(live_grid[None, :, :, None], spread, 0.0)
        columns = jnp.zeros((batch_rows, lanes * per_lane, 128), jnp.float32)
        columns = columns.at[:, flat_cols, :].add(spread.reshape(batch_rows, -1, 128))
        rounded = columns.astype(jnp.bfloat16).astype(jnp.float32)
        own_cols = rounded[:, : lanes * own_tiles].reshape(batch_rows, -1)
        border_cols = rounded[:, lanes * own_tiles :].reshape(batch_rows, -1)
        border = lax.psum_scatter(border_cols, ROW, scatter_dimension=1, tiled=True)
        returned = from_each_region(border.reshape(batch_rows, groups, -1), me)
        own_part = lax.psum_scatter(own_cols, ROW, scatter_dimension=1, tiled=True)
        through = own_part.at[:, chosen].add(returned)
        total_signed = through + jnp.dot(coeffs_b, v_factor, preferred_element_type=jnp.float32)
        grad_u = grad_u + jnp.dot(latent_b.T, scaled_b, preferred_element_type=jnp.float32)
        grad_v = grad_v + jnp.dot(coeffs_b.T, signed, preferred_element_type=jnp.float32)
        adjoint = (1.0 - leak) * adjoint + (1.0 - rates * rates) * polarity * total_signed
    return (state, grad_u, grad_v)


def solution(mesh):
    finer = Mesh(
        mesh.devices.reshape(mesh.shape["region"], 4, 4, 2), ("region", "row_0", "row_1", "row_2")
    )
    in_specs = (
        P(None, REGION_ROW),
        P(None, REGION_ROW),
        P(None, REGION_ROW),
        P(REGION_ROW),
        P(REGION_ROW, None, None, None),
        P(REGION_ROW, None),
        P(REGION_ROW),
        P("region", ROW, None, None),
        P(None, REGION_ROW),
        P(None, REGION_ROW),
    )
    out_specs = (P(None, REGION_ROW), P(None, REGION_ROW), P(None, REGION_ROW))
    return jax.shard_map(local, mesh=finer, in_specs=in_specs, out_specs=out_specs, check_vma=False)
```

profile of v0, /device:TPU:1, one launch (start us, length us, event | category | flops | bytes accessed | tf_op | source)
XLA Modules:
  0.0 1002.2 jit_solution(16985678666152582495)
XLA Ops:
  12.2 23.3 %all_gather.46 = bf16[8,32,8,16]{1,3,2,0:T(8,128)(2,1)S(1)} all-gather(bf16[1,32,8,16]{1,3,2,0:T(8,128)(2,1)S(1)} %bitcast.256), channel_id=1, replica_groups=mesh['region'=8,'row_0'=4,'row_1'=4,'row_2'=2] {'region'}, dimensions={0}, use_global_device_ids=true | all-gather | bytes 73728 | tf_op jit(solution)/shard_map/all_gather | solution.py:23
  38.0 81.1 %psum.56 = bf16[32,32]{1,0:T(8,128)(2,1)S(1)} all-reduce(f32[32,32]{1,0:T(8,128)S(1)} %fusion.61), channel_id=1, replica_groups=mesh['region'=8,'row_0'=4,'row_1'=4,'row_2'=2] {'region','row_0','row_1'..., use_global_device_ids=true, to_apply=%region_1.3 | all-reduce | flops 1024 | bytes 6144 | tf_op jit(solution)/shard_map/psum | solution.py:71
  119.2 24.4 %all_gather.47 = bf16[32,4096]{1,0:T(8,128)(2,1)S(1)} all-gather(bf16[32,128]{1,0:T(8,128)(2,1)S(1)} %copy.91), channel_id=1, replica_groups=mesh['region'=8,'row_0'=4,'row_1'=4,'row_2'=2] {'row_0','row_1','row_2'}, dimensions={1}, use_global_device_ids=true | all-gather | bytes 270336 | tf_op jit(solution)/shard_map/all_gather | solution.py:74
  143.6 2.5 copy_bitcast_fusion.6
  146.1 2.9 gather_fusion
  149.0 4.1 fusion.18
  155.6 1.7 convolution_select_fusion.2
  157.3 1.8 broadcast.101.clone
  159.1 13.2 %scatter_fusion = f32[32,160,128]{2,0,1:T(8,128)} fusion(f32[32,160,128]{2,0,1:T(8,128)} %broadcast.101.clone, s32[96]{0:T(128)S(1)} %fusion.53, f32[96,32,128]{2,1,0:T(8,128)} %bitcast.243), kind=kCustom, calls=%fused_computation.8 | custom fusion | flops 393216 | bytes 4718976 | tf_op jit(solution)/shard_map/scatter-add | solution.py:100
  172.4 2.0 convert_convert_fusion.2
  176.7 3.1 copy_bitcast_fusion.2
  181.5 19.1 %all_gather.49 = bf16[8,32,8,16]{1,3,2,0:T(8,128)(2,1)S(1)} all-gather(bf16[1,32,8,16]{1,3,2,0:T(8,128)(2,1)S(1)} %bitcast.257), channel_id=1, replica_groups=mesh['region'=8,'row_0'=4,'row_1'=4,'row_2'=2] {'region'}, dimensions={0}, use_global_device_ids=true | all-gather | bytes 73728 | tf_op jit(solution)/shard_map/all_gather | solution.py:23
  201.4 77.0 %psum.57 = bf16[32,32]{1,0:T(8,128)(2,1)} all-reduce(f32[32,32]{1,0:T(8,128)S(1)} %fusion.62), channel_id=1, replica_groups=mesh['region'=8,'row_0'=4,'row_1'=4,'row_2'=2] {'region','row_0','row_1'..., use_global_device_ids=true, to_apply=%region_3.5 | all-reduce | flops 1024 | bytes 6144 | tf_op jit(solution)/shard_map/psum | solution.py:71
  278.4 24.3 %all_gather.50 = bf16[32,4096]{1,0:T(8,128)(2,1)S(1)} all-gather(bf16[32,128]{1,0:T(8,128)(2,1)} %copy.95), channel_id=1, replica_groups=mesh['region'=8,'row_0'=4,'row_1'=4,'row_2'=2] {'row_0','row_1','row_2'}, dimensions={1}, use_global_device_ids=true | all-gather | bytes 270336 | tf_op jit(solution)/shard_map/all_gather | solution.py:74
  302.8 2.5 copy_bitcast_fusion.5
  305.3 3.0 gather_fusion.1
  308.4 4.2 fusion.16
  317.1 19.2 %all_gather.57 = f32[8,32,8,16]{1,3,2,0:T(8,128)S(1)} all-gather(f32[1,32,8,16]{1,3,2,0:T(8,128)S(1)} %bitcast.249), channel_id=1, replica_groups=mesh['region'=8,'row_0'=4,'row_1'=4,'row_2'=2] {'region'}, dimensions={0}, use_global_device_ids=true | all-gather | bytes 147456 | tf_op jit(solution)/shard_map/all_gather | solution.py:23
  338.7 19.3 %all_gather.52 = bf16[8,32,8,16]{1,3,2,0:T(8,128)(2,1)S(1)} all-gather(bf16[1,32,8,16]{1,3,2,0:T(8,128)(2,1)S(1)} %bitcast.258), channel_id=1, replica_groups=mesh['region'=8,'row_0'=4,'row_1'=4,'row_2'=2] {'region'}, dimensions={0}, use_global_device_ids=true | all-gather | bytes 73728 | tf_op jit(solution)/shard_map/all_gather | solution.py:23
  360.9 83.6 %all-reduce.1 = (bf16[32,32]{1,0:T(8,128)(2,1)}, bf16[32,32]{1,0:T(8,128)(2,1)S(1)}) all-reduce(f32[32,32]{1,0:T(8,128)S(1)} %fusion.63, f32[32,32]{1,0:T(8,128)} %fusion.65), channel_id=1, replica_groups=mesh['region'=8,'row_0'=4,'row_1'=4,'row_2'=2] {'region','row_0','row_1'..., use_global_device_ids=true, to_apply=%region_5.7 | all-reduce | flops 2048 | bytes 12288 | tf_op jit(solution)/shard_map/psum | solution.py:71
  447.7 1.9 scatter_fusion.1
  450.3 24.4 %all_gather.53 = bf16[32,4096]{1,0:T(8,128)(2,1)S(1)} all-gather(bf16[32,128]{1,0:T(8,128)(2,1)} %copy.99), channel_id=1, replica_groups=mesh['region'=8,'row_0'=4,'row_1'=4,'row_2'=2] {'row_0','row_1','row_2'}, dimensions={1}, use_global_device_ids=true | all-gather | bytes 270336 | tf_op jit(solution)/shard_map/all_gather | solution.py:74
  474.7 2.5 copy_bitcast_fusion.4
  477.2 3.0 gather_fusion.2
  480.2 4.1 fusion.14
  487.4 2.3 convolution_select_fusion.1
  489.7 1.8 broadcast.101.clone.1
  491.6 13.2 %scatter_fusion.2 = f32[32,160,128]{2,0,1:T(8,128)} fusion(f32[32,160,128]{2,0,1:T(8,128)} %broadcast.101.clone.1, s32[96]{0:T(128)S(1)} %copy-done.35, f32[96,32,128]{2,1,0:T(8,128)} %bitcast.244), kind=kCustom, calls=%fused_computation.10 | custom fusion | flops 393216 | bytes 4718976 | tf_op jit(solution)/shard_map/scatter-add | solution.py:100
  504.7 2.0 convert_convert_fusion.1
  509.1 3.1 copy_bitcast_fusion.1
  512.4 73.7 %psum.61 = bf16[32,32]{1,0:T(8,128)(2,1)S(1)} all-reduce(f32[32,32]{1,0:T(8,128)S(1)} %fusion.66), channel_id=1, replica_groups=mesh['region'=8,'row_0'=4,'row_1'=4,'row_2'=2] {'region','row_0','row_1'..., use_global_device_ids=true, to_apply=%region_15.17 | all-reduce | flops 1024 | bytes 6144 | tf_op jit(solution)/shard_map/psum | solution.py:87
  588.7 21.2 %all_gather.58 = f32[8,32,8,16]{1,3,2,0:T(8,128)S(1)} all-gather(f32[1,32,8,16]{1,3,2,0:T(8,128)S(1)} %bitcast.250), channel_id=1, replica_groups=mesh['region'=8,'row_0'=4,'row_1'=4,'row_2'=2] {'region'}, dimensions={0}, use_global_device_ids=true | all-gather | bytes 147456 | tf_op jit(solution)/shard_map/all_gather | solution.py:23
  610.5 67.1 %reduce-scatter.11.cloned.1.call-done = f32[32,512]{1,0:T(8,128)} async-done(((f32[32,16384]{1,0:T(8,128)}), f32[32,512]{1,0:T(8,128)}) %reduce-scatter.11.cloned.1.call-update) | async-done | bytes 65552 | tf_op jit(solution)/shard_map/reduce_scatter | solution.py:106
  683.5 2.3 convolution_select_fusion
  685.8 1.8 broadcast.101
  687.6 13.2 %scatter_fusion.4 = f32[32,160,128]{2,0,1:T(8,128)} fusion(f32[32,160,128]{2,0,1:T(8,128)} %broadcast.101, s32[96]{0:T(128)S(1)} %copy-done.36, f32[96,32,128]{2,1,0:T(8,128)} %bitcast.242), kind=kCustom, calls=%fused_computation.12 | custom fusion | flops 393216 | bytes 4718976 | tf_op jit(solution)/shard_map/scatter-add | solution.py:100
  700.8 2.0 convert_convert_fusion
  705.2 3.1 copy_bitcast_fusion
  710.0 20.6 %all_gather.55 = bf16[8,32,8,16]{1,3,2,0:T(8,128)(2,1)S(1)} all-gather(bf16[1,32,8,16]{1,3,2,0:T(8,128)(2,1)S(1)} %bitcast.255), channel_id=1, replica_groups=mesh['region'=8,'row_0'=4,'row_1'=4,'row_2'=2] {'region'}, dimensions={0}, use_global_device_ids=true | all-gather | bytes 73728 | tf_op jit(solution)/shard_map/all_gather | solution.py:23
  732.6 31.8 %all_gather.56 = bf16[32,4096]{1,0:T(8,128)(2,1)S(1)} all-gather(bf16[32,128]{1,0:T(8,128)(2,1)} %copy.103), channel_id=1, replica_groups=mesh['region'=8,'row_0'=4,'row_1'=4,'row_2'=2] {'row_0','row_1','row_2'}, dimensions={1}, use_global_device_ids=true | all-gather | bytes 270336 | tf_op jit(solution)/shard_map/all_gather | solution.py:74
  768.4 2.5 copy_bitcast_fusion.3
  770.9 3.0 gather_fusion.3
  774.0 4.1 fusion.12
  778.1 2.1 reduce_sum.39
  780.3 74.4 %psum.62 = bf16[32,32]{1,0:T(8,128)(2,1)S(1)} all-reduce(f32[32,32]{1,0:T(8,128)S(1)} %fusion.67), channel_id=1, replica_groups=mesh['region'=8,'row_0'=4,'row_1'=4,'row_2'=2] {'region','row_0','row_1'..., use_global_device_ids=true, to_apply=%region_20.22 | all-reduce | flops 1024 | bytes 6144 | tf_op jit(solution)/shard_map/psum | solution.py:87
  856.4 19.5 %all_gather.59 = f32[8,32,8,16]{1,3,2,0:T(8,128)S(1)} all-gather(f32[1,32,8,16]{1,3,2,0:T(8,128)S(1)} %bitcast.251), channel_id=1, replica_groups=mesh['region'=8,'row_0'=4,'row_1'=4,'row_2'=2] {'region'}, dimensions={0}, use_global_device_ids=true | all-gather | bytes 147456 | tf_op jit(solution)/shard_map/all_gather | solution.py:23
  876.5 28.5 %reduce-scatter.15.cloned.1.call-done = f32[32,512]{1,0:T(8,128)} async-done(((f32[32,16384]{1,0:T(8,128)}), f32[32,512]{1,0:T(8,128)}) %reduce-scatter.15.cloned.1.call-update) | async-done | bytes 65552 | tf_op jit(solution)/shard_map/reduce_scatter | solution.py:106
  911.1 77.4 %all-reduce = (bf16[32,32]{1,0:T(8,128)(2,1)S(1)}, bf16[32,32]{1,0:T(8,128)(2,1)S(1)}) all-reduce(f32[32,32]{1,0:T(8,128)} %fusion.64, f32[32,32]{1,0:T(8,128)S(1)} %fusion.68), channel_id=1, replica_groups=mesh['region'=8,'row_0'=4,'row_1'=4,'row_2'=2] {'region','row_0','row_1'..., use_global_device_ids=true, to_apply=%region_7.9 | all-reduce | flops 2048 | bytes 12288 | tf_op jit(solution)/shard_map/psum | solution.py:71
  (189 shorter events, 68.7 us)
Async XLA Ops:
  7.2 141.8 %copy-start = (bf16[4,24,128,128]{3,2,1,0:T(8,128)(2,1)S(1)}, bf16[4,24,128,128]{3,2,1,0:T(8,128)(2,1)}, u32[]{:S(2)}) copy-start(bf16[4,24,128,128]{3,2,1,0:T(8,128)(2,1)} %param.16) | copy-start | bytes 9437188
  7.2 136.4 %all-gather.5.cloned.1.call-start = ((), (), s32[]{:S(2)}) async-start(), calls=%async_computation.6 | async-start | bytes 1081344 | tf_op jit(solution)/shard_map/all_gather | solution.py:68
  9.6 293.2 %all-gather.7.cloned.1.call-start = ((), (), s32[]{:S(2)}) async-start(), calls=%async_computation.7 | async-start | bytes 1081344 | tf_op jit(solution)/shard_map/all_gather | solution.py:68
  12.1 169.3 %copy-start.31 = (pred[128]{0:T(512)(128)(4,1)}, pred[128]{0:T(512)(128)(4,1)S(1)}, u32[]{:S(2)}) copy-start(pred[128]{0:T(512)(128)(4,1)S(1)} %compare_and_fusion) | copy-start | bytes 388
  37.1 118.5 %copy-start.37 = (pred[4,24]{1,0:T(4,128)(4,1)}, pred[4,24]{1,0:T(4,128)(4,1)S(1)}, u32[]{:S(2)}) copy-start(pred[4,24]{1,0:T(4,128)(4,1)S(1)} %iota_compare_fusion) | copy-start | bytes 292
  37.1 111.8 %copy-start.28 = (pred[96]{0:T(512)(128)(4,1)}, pred[96]{0:T(512)(128)(4,1)S(1)}, u32[]{:S(2)}) copy-start(pred[96]{0:T(512)(128)(4,1)S(1)} %lt.81) | copy-start | bytes 292
  143.5 15.6 %copy-start.34 = (s32[96]{0:T(128)}, s32[96]{0:T(128)S(1)}, u32[]{:S(2)}) copy-start(s32[96]{0:T(128)S(1)} %fusion.53) | copy-start | bytes 1156
  143.5 5.4 copy-start.27
  149.0 5.7 copy-start.4
  149.0 5.7 copy-start.10
  149.0 5.7 copy-start.18
  149.0 6.5 copy-start.21
  155.5 160.8 %reduce-scatter.9.cloned.1.call-start = ((), (), s32[]{:S(2)}) async-start(), calls=%async_computation.11 | async-start | bytes 540672 | tf_op jit(solution)/shard_map/reduce_scatter | solution.py:104
  155.6 1.7 copy-start.13
  174.3 1.5 copy-start.1
  176.7 267.8 %reduce-scatter.7.cloned.1.call-start = ((), (), s32[]{:S(2)}) async-start(), calls=%async_computation.10 | async-start | bytes 2162688 | tf_op jit(solution)/shard_map/reduce_scatter | solution.py:106
  179.8 0.8 copy-start.6
  179.8 21.5 %copy-start.5 = (bf16[32,512]{1,0:T(8,128)(2,1)S(1)}, bf16[32,512]{1,0:T(8,128)(2,1)}, u32[]{:S(2)}) copy-start(bf16[32,512]{1,0:T(8,128)(2,1)} %param.21) | copy-start | bytes 98308
  179.8 294.9 %all-gather.9.cloned.1.call-start = ((), (), s32[]{:S(2)}) async-start(), calls=%async_computation.8 | async-start | bytes 1081344 | tf_op jit(solution)/shard_map/all_gather | solution.py:68
  302.8 5.6 copy-start.29
  308.4 5.7 copy-start.9
  308.4 5.7 copy-start.11
  308.4 5.7 copy-start.23
  308.4 6.6 copy-start.26
  308.4 7.2 copy-start.14
  312.5 26.0 %copy-start.32 = (pred[128]{0:T(512)(128)(4,1)S(1)}, pred[128]{0:T(512)(128)(4,1)}, u32[]{:S(2)}) copy-start(pred[128]{0:T(512)(128)(4,1)} %copy-done.31) | copy-start | bytes 388
  314.9 273.0 %reduce-scatter.13.cloned.1.call-start = ((), (), s32[]{:S(2)}) async-start(), calls=%async_computation.13 | async-start | bytes 540672 | tf_op jit(solution)/shard_map/reduce_scatter | solution.py:104
  480.2 5.6 copy-start.12
  480.2 5.6 copy-start.20
  480.2 5.7 copy-start.22
  487.4 24.9 %copy-start.15 = (bf16[32,512]{1,0:T(8,128)(2,1)}, bf16[32,512]{1,0:T(8,128)(2,1)S(1)}, u32[]{:S(2)}) copy-start(bf16[32,512]{1,0:T(8,128)(2,1)S(1)} %get-tuple-element.8) | copy-start | bytes 98308
  489.7 1.9 copy-start.35
  506.7 1.5 copy-start.2
  509.1 168.5 %reduce-scatter.11.cloned.1.call-start = ((), (), s32[]{:S(2)}) async-start(), calls=%async_computation.12 | async-start | bytes 2162688 | tf_op jit(solution)/shard_map/reduce_scatter | solution.py:106
  512.2 256.2 %all-gather.11.cloned.1.call-start = ((), (), s32[]{:S(2)}) async-start(), calls=%async_computation.9 | async-start | bytes 1081344 | tf_op jit(solution)/shard_map/all_gather | solution.py:68
  586.1 91.5 %copy-start.24 = (bf16[32,32]{1,0:T(8,128)(2,1)}, bf16[32,32]{1,0:T(8,128)(2,1)S(1)}, u32[]{:S(2)}) copy-start(bf16[32,32]{1,0:T(8,128)(2,1)S(1)} %psum.61) | copy-start | bytes 6148
  586.2 269.4 %reduce-scatter.17.cloned.1.call-start = ((), (), s32[]{:S(2)}) async-start(), calls=%async_computation.15 | async-start | bytes 540672 | tf_op jit(solution)/shard_map/reduce_scatter | solution.py:104
  683.5 2.3 copy-start.16
  685.8 1.9 copy-start.36
  702.8 1.5 copy-start.3
  705.2 199.8 %reduce-scatter.15.cloned.1.call-start = ((), (), s32[]{:S(2)}) async-start(), calls=%async_computation.14 | async-start | bytes 2162688 | tf_op jit(solution)/shard_map/reduce_scatter | solution.py:106
  708.3 0.8 copy-start.8
  708.3 1.6 copy-start.33
  768.4 5.5 copy-start.30
  773.9 6.3 copy-start.17
  773.9 80.8 %copy-start.7 = (bf16[32,512]{1,0:T(8,128)(2,1)S(1)}, bf16[32,512]{1,0:T(8,128)(2,1)}, u32[]{:S(2)}) copy-start(bf16[32,512]{1,0:T(8,128)(2,1)} %get-tuple-element.11) | copy-start | bytes 98308
  774.0 80.8 %copy-start.19 = (f32[32,512]{1,0:T(8,128)S(1)}, f32[32,512]{1,0:T(8,128)}, u32[]{:S(2)}) copy-start(f32[32,512]{1,0:T(8,128)} %convolution_add_fusion.2) | copy-start | bytes 196612
  778.1 129.5 %copy-start.38 = (s32[128]{0:T(128)S(1)}, s32[128]{0:T(128)}, u32[]{:S(2)}) copy-start(s32[128]{0:T(128)} %fusion.54) | copy-start | bytes 1540
  (1 other events, 0.6 us)
Sparse Core Ops, SparseCore 0:
  10.5 52.4 all-gather.4
  155.6 44.2 all-gather.6
  203.6 81.8 reduce-scatter.8
  289.2 85.9 reduce-scatter.6
  377.6 49.4 all-gather.8
  509.2 78.6 reduce-scatter.12
  591.7 85.8 reduce-scatter.10
  680.1 49.4 all-gather.10
  733.3 82.0 reduce-scatter.16
  819.1 85.8 reduce-scatter.14
where the time goes:
time: 1010 us; the launch traced here: 1000 us
  blocking collectives  714 us (71%)
  waiting for transfers between devices  97.5 us (10%)
  other arithmetic  74.2 us (7%)
  local copies, waits for them, and re-layouts  56 us (6%)
  matrix products  45.3 us (4%)
  between operations  14.6 us (1%)
    psum x4, blocking collectives, local(): lax.psum(jnp.dot(signed, v_factor.T, preferred_element_type=jnp.float32),...  319 us
    psum x2, blocking collectives, local(): lax.psum(jnp.dot(scaled_b, u_factor.T, preferred_element_type=jnp.float32...  148 us
    all_gather x7, blocking collectives, from_each_region(): everyone = lax.all_gather(x, 'region', axis=0, tiled=False)  142 us
    all_gather x4, blocking collectives, local(): gathered_border = lax.all_gather(incoming, ROW, axis=1, tiled=True)  105 us
    reduce_scatter x3, waiting for transfers between devices, local(): own_part = lax.psum_scatter(own_cols, ROW, scatter_dimension=1, tiled=True)  95.6 us
    scatter-add x3, other arithmetic, local(): columns.at[:, flat_cols, :].add(spread.reshape(batch_rows, -1, 128))  39.6 us
  transfers between devices with their start and end apart: 10, of which 3 were waited for; matrix products, arithmetic and copies ran while one was open for 11% of the time, Pallas kernels for 0%

commit v1 on v0

--- a/solution.py
+++ b/solution.py
@@ -8,6 +8,13 @@
 ROW = ("row_0", "row_1", "row_2")
 REGION_ROW = ("region", "row_0", "row_1", "row_2")
 leak = 0.5
+
+
+def gather_over(shard, name, dim):
+    size = lax.axis_size(name)
+    tiles = jnp.stack([shard for _ in range(size)])
+    tiles = lax.all_to_all(tiles, name, split_axis=0, concat_axis=0)
+    return jnp.concatenate(tiles, axis=dim)
 
 
 def apply_tiles(ext_cols, flat_cols, live_tiles, flat_tiles, row_tiles):
@@ -71,7 +78,7 @@
         latent = lax.psum(
             jnp.dot(signed, v_factor.T, preferred_element_type=jnp.float32), REGION_ROW
         )
-        gathered_border = lax.all_gather(incoming, ROW, axis=1, tiled=True)
+        gathered_border = gather_over(incoming, ROW, 1)
         gathered = jnp.concatenate([gathered_own, gathered_border], axis=1)
         synaptic = apply_tiles(gathered, flat_cols, live_tiles, flat_tiles, row_tiles)
         latent_b = latent.astype(jnp.bfloat16)

time: 1010 us -> 965 us (0.955)
  blocking collectives: 714 us -> 597 us
  starting transfers between devices: 0.41 us -> 55.3 us
  waiting for transfers between devices: 97.5 us -> 120 us
    all_gather x4 -> x0, blocking collectives: 105 us -> none  [local(): gathered_border = lax.all_gather(incoming, ROW, axis=1, tiled=True)]
    all_to_all x0 -> x4, starting transfers between devices: none -> 54.9 us  [gather_over(): tiles = lax.all_to_all(tiles, name, split_axis=0, concat_axis=0)]
    reduce_scatter x3, waiting for transfers between devices: 95.6 us -> 110 us  [local(): own_part = lax.psum_scatter(own_cols, ROW, scatter_dimension=1, tiled=True)]
    psum x4, blocking collectives: 319 us -> 307 us  [local(): lax.psum(jnp.dot(signed, v_factor.T, preferred_element_type=jnp.float32),...]
  transfers between devices with their start and end apart: 10 -> 14, of which waited for: 3 -> 4; matrix products, arithmetic and copies ran while one was open for 11% -> 11% of each run, Pallas kernels for 0% -> 0%
where the time goes in v1:
time: 965 us; the launch traced here: 962 us
  blocking collectives  597 us (62%)
  waiting for transfers between devices  120 us (12%)
  other arithmetic  74 us (8%)
  local copies, waits for them, and re-layouts  58.9 us (6%)
  starting transfers between devices  55.3 us (6%)
  matrix products  42.3 us (4%)
  between operations  14.8 us (2%)
    psum x4, blocking collectives, local(): lax.psum(jnp.dot(signed, v_factor.T, preferred_element_type=jnp.float32),...  307 us
    psum x2, blocking collectives, local(): lax.psum(jnp.dot(scaled_b, u_factor.T, preferred_element_type=jnp.float32...  148 us
    all_gather x7, blocking collectives, from_each_region(): everyone = lax.all_gather(x, 'region', axis=0, tiled=False)  142 us
    reduce_scatter x3, waiting for transfers between devices, local(): own_part = lax.psum_scatter(own_cols, ROW, scatter_dimension=1, tiled=True)  110 us
    all_to_all x4, starting transfers between devices, gather_over(): tiles = lax.all_to_all(tiles, name, split_axis=0, concat_axis=0)  54.9 us
    scatter-add x3, other arithmetic, local(): columns.at[:, flat_cols, :].add(spread.reshape(batch_rows, -1, 128))  39.6 us
  transfers between devices with their start and end apart: 14, of which 4 were waited for; matrix products, arithmetic and copies ran while one was open for 11% of the time, Pallas kernels for 0%

profile of v1, /device:TPU:1, one launch (start us, length us, event | category | flops | bytes accessed | tf_op | source)
XLA Modules:
  0.0 962.0 jit_solution(1568649331610203075)
XLA Ops:
  12.1 23.3 %all_gather.34 = bf16[8,32,8,16]{1,3,2,0:T(8,128)(2,1)S(1)} all-gather(bf16[1,32,8,16]{1,3,2,0:T(8,128)(2,1)S(1)} %bitcast.280), channel_id=1, replica_groups=mesh['region'=8,'row_0'=4,'row_1'=4,'row_2'=2] {'region'}, dimensions={0}, use_global_device_ids=true | all-gather | bytes 73728 | tf_op jit(solution)/shard_map/all_gather | solution.py:30
  36.2 13.9 %all-to-all-start = ((bf16[32,32,128]{2,1,0:T(8,128)(2,1)}), bf16[32,32,128]{2,1,0:T(8,128)(2,1)}, u32[]{:S(2)}, u32[]{:S(2)}) async-start(bf16[32,32,128]{2,1,0:T(8,128)(2,1)} %stack.12), calls=%async_computation | async-start | bytes 524288 | tf_op jit(solution)/shard_map/all_to_all | solution.py:16
  52.7 76.7 %psum.56 = bf16[32,32]{1,0:T(8,128)(2,1)S(1)} all-reduce(f32[32,32]{1,0:T(8,128)S(1)} %fusion.61), channel_id=1, replica_groups=mesh['region'=8,'row_0'=4,'row_1'=4,'row_2'=2] {'region','row_0','row_1'..., use_global_device_ids=true, to_apply=%region_1.3 | all-reduce | flops 1024 | bytes 6144 | tf_op jit(solution)/shard_map/psum | solution.py:78
  130.4 2.5 copy_bitcast_fusion.6
  133.0 2.9 gather_fusion
  135.9 4.1 fusion.18
  144.2 1.8 broadcast.105.clone
  146.0 13.2 %scatter_fusion = f32[32,160,128]{2,0,1:T(8,128)} fusion(f32[32,160,128]{2,0,1:T(8,128)} %broadcast.105.clone, s32[96]{0:T(128)S(1)} %fusion.53, f32[96,32,128]{2,1,0:T(8,128)} %bitcast.267), kind=kCustom, calls=%fused_computation.8 | custom fusion | flops 393216 | bytes 4718976 | tf_op jit(solution)/shard_map/scatter-add | solution.py:107
  159.2 2.0 convert_convert_fusion.2
  163.6 3.1 copy_bitcast_fusion.2
  168.4 19.1 %all_gather.36 = bf16[8,32,8,16]{1,3,2,0:T(8,128)(2,1)S(1)} all-gather(bf16[1,32,8,16]{1,3,2,0:T(8,128)(2,1)S(1)} %bitcast.281), channel_id=1, replica_groups=mesh['region'=8,'row_0'=4,'row_1'=4,'row_2'=2] {'region'}, dimensions={0}, use_global_device_ids=true | all-gather | bytes 73728 | tf_op jit(solution)/shard_map/all_gather | solution.py:30
  188.4 11.0 %all-to-all-start.1 = ((bf16[32,32,128]{2,1,0:T(8,128)(2,1)}), bf16[32,32,128]{2,1,0:T(8,128)(2,1)}, u32[]{:S(2)}, u32[]{:S(2)}) async-start(bf16[32,32,128]{2,1,0:T(8,128)(2,1)} %stack.13), calls=%async_computation.1 | async-start | bytes 524288 | tf_op jit(solution)/shard_map/all_to_all | solution.py:16
  200.9 76.8 %psum.57 = bf16[32,32]{1,0:T(8,128)(2,1)} all-reduce(f32[32,32]{1,0:T(8,128)S(1)} %fusion.62), channel_id=1, replica_groups=mesh['region'=8,'row_0'=4,'row_1'=4,'row_2'=2] {'region','row_0','row_1'..., use_global_device_ids=true, to_apply=%region_3.5 | all-reduce | flops 1024 | bytes 6144 | tf_op jit(solution)/shard_map/psum | solution.py:78
  278.6 2.5 copy_bitcast_fusion.5
  281.2 3.0 gather_fusion.1
  284.2 4.1 fusion.16
  292.1 19.3 %all_gather.41 = f32[8,32,8,16]{1,3,2,0:T(8,128)S(1)} all-gather(f32[1,32,8,16]{1,3,2,0:T(8,128)S(1)} %bitcast.273), channel_id=1, replica_groups=mesh['region'=8,'row_0'=4,'row_1'=4,'row_2'=2] {'region'}, dimensions={0}, use_global_device_ids=true | all-gather | bytes 147456 | tf_op jit(solution)/shard_map/all_gather | solution.py:30
  313.7 18.9 %all_gather.38 = bf16[8,32,8,16]{1,3,2,0:T(8,128)(2,1)S(1)} all-gather(bf16[1,32,8,16]{1,3,2,0:T(8,128)(2,1)S(1)} %bitcast.282), channel_id=1, replica_groups=mesh['region'=8,'row_0'=4,'row_1'=4,'row_2'=2] {'region'}, dimensions={0}, use_global_device_ids=true | all-gather | bytes 73728 | tf_op jit(solution)/shard_map/all_gather | solution.py:30
  333.4 16.9 %all-to-all-start.2 = ((bf16[32,32,128]{2,1,0:T(8,128)(2,1)}), bf16[32,32,128]{2,1,0:T(8,128)(2,1)}, u32[]{:S(2)}, u32[]{:S(2)}) async-start(bf16[32,32,128]{2,1,0:T(8,128)(2,1)} %stack.14), calls=%async_computation.2 | async-start | bytes 524288 | tf_op jit(solution)/shard_map/all_to_all | solution.py:16
  350.5 76.5 %all-reduce.1 = (bf16[32,32]{1,0:T(8,128)(2,1)}, bf16[32,32]{1,0:T(8,128)(2,1)S(1)}) all-reduce(f32[32,32]{1,0:T(8,128)S(1)} %fusion.63, f32[32,32]{1,0:T(8,128)S(1)} %copy-done.27), channel_id=1, replica_groups=mesh['region'=8,'row_0'=4,'row_1'=4,'row_2'=2] {'region','row_0','row_1'..., use_global_device_ids=true, to_apply=%region_5.7 | all-reduce | flops 2048 | bytes 12288 | tf_op jit(solution)/shard_map/psum | solution.py:78
  433.6 2.5 copy_bitcast_fusion.4
  436.2 3.0 gather_fusion.2
  439.2 4.1 fusion.14
  446.4 2.3 convolution_select_fusion.1
  448.7 1.8 broadcast.105.clone.1
  450.5 13.2 %scatter_fusion.2 = f32[32,160,128]{2,0,1:T(8,128)} fusion(f32[32,160,128]{2,0,1:T(8,128)} %broadcast.105.clone.1, s32[96]{0:T(128)S(1)} %copy-done.40, f32[96,32,128]{2,1,0:T(8,128)} %bitcast.268), kind=kCustom, calls=%fused_computation.10 | custom fusion | flops 393216 | bytes 4718976 | tf_op jit(solution)/shard_map/scatter-add | solution.py:107
  463.7 2.0 convert_convert_fusion.1
  468.1 3.1 copy_bitcast_fusion.1
  471.4 74.2 %psum.61 = bf16[32,32]{1,0:T(8,128)(2,1)S(1)} all-reduce(f32[32,32]{1,0:T(8,128)S(1)} %fusion.66), channel_id=1, replica_groups=mesh['region'=8,'row_0'=4,'row_1'=4,'row_2'=2] {'region','row_0','row_1'..., use_global_device_ids=true, to_apply=%region_15.17 | all-reduce | flops 1024 | bytes 6144 | tf_op jit(solution)/shard_map/psum | solution.py:94
  545.7 1.9 reduce-scatter.13.cloned.1.call-done
  548.4 21.2 %all_gather.42 = f32[8,32,8,16]{1,3,2,0:T(8,128)S(1)} all-gather(f32[1,32,8,16]{1,3,2,0:T(8,128)S(1)} %bitcast.274), channel_id=1, replica_groups=mesh['region'=8,'row_0'=4,'row_1'=4,'row_2'=2] {'region'}, dimensions={0}, use_global_device_ids=true | all-gather | bytes 147456 | tf_op jit(solution)/shard_map/all_gather | solution.py:30
  570.3 67.0 %reduce-scatter.11.cloned.1.call-done = f32[32,512]{1,0:T(8,128)} async-done(((f32[32,16384]{1,0:T(8,128)}), f32[32,512]{1,0:T(8,128)}) %reduce-scatter.11.cloned.1.call-update) | async-done | bytes 65552 | tf_op jit(solution)/shard_map/reduce_scatter | solution.py:113
  643.2 2.3 convolution_select_fusion
  645.5 1.8 broadcast.105
  647.3 13.2 %scatter_fusion.4 = f32[32,160,128]{2,0,1:T(8,128)} fusion(f32[32,160,128]{2,0,1:T(8,128)} %broadcast.105, s32[96]{0:T(128)S(1)} %copy-done.41, f32[96,32,128]{2,1,0:T(8,128)} %bitcast.266), kind=kCustom, calls=%fused_computation.12 | custom fusion | flops 393216 | bytes 4718976 | tf_op jit(solution)/shard_map/scatter-add | solution.py:107
  660.5 2.0 convert_convert_fusion
  664.9 3.1 copy_bitcast_fusion
  669.7 20.5 %all_gather.40 = bf16[8,32,8,16]{1,3,2,0:T(8,128)(2,1)S(1)} all-gather(bf16[1,32,8,16]{1,3,2,0:T(8,128)(2,1)S(1)} %bitcast.279), channel_id=1, replica_groups=mesh['region'=8,'row_0'=4,'row_1'=4,'row_2'=2] {'region'}, dimensions={0}, use_global_device_ids=true | all-gather | bytes 73728 | tf_op jit(solution)/shard_map/all_gather | solution.py:30
  691.0 13.1 %all-to-all-start.3 = ((bf16[32,32,128]{2,1,0:T(8,128)(2,1)}), bf16[32,32,128]{2,1,0:T(8,128)(2,1)}, u32[]{:S(2)}, u32[]{:S(2)}) async-start(bf16[32,32,128]{2,1,0:T(8,128)(2,1)} %stack.15), calls=%async_computation.3 | async-start | bytes 524288 | tf_op jit(solution)/shard_map/all_to_all | solution.py:16
  705.9 7.2 all-to-all-done.3
  714.1 2.5 copy_bitcast_fusion.3
  716.7 3.0 gather_fusion.3
  719.7 4.1 fusion.12
  723.8 2.2 reduce_sum.39
  726.1 73.8 %psum.62 = bf16[32,32]{1,0:T(8,128)(2,1)S(1)} all-reduce(f32[32,32]{1,0:T(8,128)S(1)} %fusion.67), channel_id=1, replica_groups=mesh['region'=8,'row_0'=4,'row_1'=4,'row_2'=2] {'region','row_0','row_1'..., use_global_device_ids=true, to_apply=%region_20.22 | all-reduce | flops 1024 | bytes 6144 | tf_op jit(solution)/shard_map/psum | solution.py:94
  801.6 19.4 %all_gather.43 = f32[8,32,8,16]{1,3,2,0:T(8,128)S(1)} all-gather(f32[1,32,8,16]{1,3,2,0:T(8,128)S(1)} %bitcast.275), channel_id=1, replica_groups=mesh['region'=8,'row_0'=4,'row_1'=4,'row_2'=2] {'region'}, dimensions={0}, use_global_device_ids=true | all-gather | bytes 147456 | tf_op jit(solution)/shard_map/all_gather | solution.py:30
  821.6 43.2 %reduce-scatter.15.cloned.1.call-done = f32[32,512]{1,0:T(8,128)} async-done(((f32[32,16384]{1,0:T(8,128)}), f32[32,512]{1,0:T(8,128)}) %reduce-scatter.15.cloned.1.call-update) | async-done | bytes 65552 | tf_op jit(solution)/shard_map/reduce_scatter | solution.py:113
  870.8 77.4 %all-reduce = (bf16[32,32]{1,0:T(8,128)(2,1)S(1)}, bf16[32,32]{1,0:T(8,128)(2,1)S(1)}) all-reduce(f32[32,32]{1,0:T(8,128)} %fusion.64, f32[32,32]{1,0:T(8,128)S(1)} %fusion.68), channel_id=1, replica_groups=mesh['region'=8,'row_0'=4,'row_1'=4,'row_2'=2] {'region','row_0','row_1'..., use_global_device_ids=true, to_apply=%region_7.9 | all-reduce | flops 2048 | bytes 12288 | tf_op jit(solution)/shard_map/psum | solution.py:78
  (213 shorter events, 70.3 us)
Async XLA Ops:
  7.2 128.7 %copy-start = (bf16[4,24,128,128]{3,2,1,0:T(8,128)(2,1)S(1)}, bf16[4,24,128,128]{3,2,1,0:T(8,128)(2,1)}, u32[]{:S(2)}) copy-start(bf16[4,24,128,128]{3,2,1,0:T(8,128)(2,1)} %param.16) | copy-start | bytes 9437188
  7.2 123.2 %all-gather.5.cloned.1.call-start = ((), (), s32[]{:S(2)}) async-start(), calls=%async_computation.10 | async-start | bytes 1081344 | tf_op jit(solution)/shard_map/all_gather | solution.py:75
  11.3 40.5 %copy-start.32 = (pred[128]{0:T(512)(128)(4,1)}, pred[128]{0:T(512)(128)(4,1)S(1)}, u32[]{:S(2)}) copy-start(pred[128]{0:T(512)(128)(4,1)S(1)} %compare_and_fusion) | copy-start | bytes 388
  36.2 93.2 %all-to-all-start = ((bf16[32,32,128]{2,1,0:T(8,128)(2,1)}), bf16[32,32,128]{2,1,0:T(8,128)(2,1)}, u32[]{:S(2)}, u32[]{:S(2)}) async-start(bf16[32,32,128]{2,1,0:T(8,128)(2,1)} %stack.12), calls=%async_computation | async-start | bytes 524288 | tf_op jit(solution)/shard_map/all_to_all | solution.py:16
  50.2 228.4 %all-gather.7.cloned.1.call-start = ((), (), s32[]{:S(2)}) async-start(), calls=%async_computation.11 | async-start | bytes 1081344 | tf_op jit(solution)/shard_map/all_gather | solution.py:75
  51.7 90.7 %copy-start.42 = (pred[4,24]{1,0:T(4,128)(4,1)}, pred[4,24]{1,0:T(4,128)(4,1)S(1)}, u32[]{:S(2)}) copy-start(pred[4,24]{1,0:T(4,128)(4,1)S(1)} %iota_compare_fusion) | copy-start | bytes 292
  51.8 84.0 %copy-start.36 = (pred[96]{0:T(512)(128)(4,1)}, pred[96]{0:T(512)(128)(4,1)S(1)}, u32[]{:S(2)}) copy-start(pred[96]{0:T(512)(128)(4,1)S(1)} %lt.81) | copy-start | bytes 292
  129.4 16.6 %copy-start.39 = (s32[96]{0:T(128)}, s32[96]{0:T(128)S(1)}, u32[]{:S(2)}) copy-start(s32[96]{0:T(128)S(1)} %fusion.53) | copy-start | bytes 1156
  129.4 6.4 copy-start.31
  135.9 5.7 copy-start.4
  135.9 5.7 copy-start.12
  135.9 5.7 copy-start.19
  135.9 6.5 copy-start.22
  142.4 148.9 %reduce-scatter.9.cloned.1.call-start = ((), (), s32[]{:S(2)}) async-start(), calls=%async_computation.15 | async-start | bytes 540672 | tf_op jit(solution)/shard_map/reduce_scatter | solution.py:111
  142.4 57.0 %copy-start.15 = (bf16[32,512]{1,0:T(8,128)(2,1)}, bf16[32,512]{1,0:T(8,128)(2,1)S(1)}, u32[]{:S(2)}) copy-start(bf16[32,512]{1,0:T(8,128)(2,1)S(1)} %multiply_convert_fusion.5) | copy-start | bytes 98308
  163.6 263.5 %reduce-scatter.7.cloned.1.call-start = ((), (), s32[]{:S(2)}) async-start(), calls=%async_computation.14 | async-start | bytes 2162688 | tf_op jit(solution)/shard_map/reduce_scatter | solution.py:113
  166.7 33.4 %copy-start.30 = (s32[1,1,8,16]{3,2,1,0:T(8,128)S(1)}, s32[1,1,8,16]{3,2,1,0:T(8,128)}, u32[]{:S(2)}) copy-start(s32[1,1,8,16]{3,2,1,0:T(8,128)} %param.19) | copy-start | bytes 1540
  166.7 34.0 %copy-start.5 = (bf16[32,512]{1,0:T(8,128)(2,1)S(1)}, bf16[32,512]{1,0:T(8,128)(2,1)}, u32[]{:S(2)}) copy-start(bf16[32,512]{1,0:T(8,128)(2,1)} %param.21) | copy-start | bytes 98308
  188.4 89.2 %all-to-all-start.1 = ((bf16[32,32,128]{2,1,0:T(8,128)(2,1)}), bf16[32,32,128]{2,1,0:T(8,128)(2,1)}, u32[]{:S(2)}, u32[]{:S(2)}) async-start(bf16[32,32,128]{2,1,0:T(8,128)(2,1)} %stack.13), calls=%async_computation.1 | async-start | bytes 524288 | tf_op jit(solution)/shard_map/all_to_all | solution.py:16
  199.3 234.3 %all-gather.9.cloned.1.call-start = ((), (), s32[]{:S(2)}) async-start(), calls=%async_computation.12 | async-start | bytes 1081344 | tf_op jit(solution)/shard_map/all_gather | solution.py:75
  278.6 5.6 copy-start.37
  284.2 5.7 copy-start.11
  284.2 5.7 copy-start.13
  284.2 5.7 copy-start.24
  284.2 6.5 copy-start.44
  288.3 25.3 %copy-start.34 = (pred[128]{0:T(512)(128)(4,1)S(1)}, pred[128]{0:T(512)(128)(4,1)}, u32[]{:S(2)}) copy-start(pred[128]{0:T(512)(128)(4,1)} %copy-done.32) | copy-start | bytes 388
  288.3 62.2 %copy-start.27 = (f32[32,32]{1,0:T(8,128)S(1)}, f32[32,32]{1,0:T(8,128)}, u32[]{:S(2)}) copy-start(f32[32,32]{1,0:T(8,128)} %fusion.65) | copy-start | bytes 12292
  290.7 59.7 %copy-start.8 = (bf16[32,512]{1,0:T(8,128)(2,1)S(1)}, bf16[32,512]{1,0:T(8,128)(2,1)}, u32[]{:S(2)}) copy-start(bf16[32,512]{1,0:T(8,128)(2,1)} %get-tuple-element.13) | copy-start | bytes 98308
  333.4 99.2 %all-to-all-start.2 = ((bf16[32,32,128]{2,1,0:T(8,128)(2,1)}), bf16[32,32,128]{2,1,0:T(8,128)(2,1)}, u32[]{:S(2)}, u32[]{:S(2)}) async-start(bf16[32,32,128]{2,1,0:T(8,128)(2,1)} %stack.14), calls=%async_computation.2 | async-start | bytes 524288 | tf_op jit(solution)/shard_map/all_to_all | solution.py:16
  350.3 197.2 %reduce-scatter.13.cloned.1.call-start = ((), (), s32[]{:S(2)}) async-start(), calls=%async_computation.17 | async-start | bytes 540672 | tf_op jit(solution)/shard_map/reduce_scatter | solution.py:111
  439.2 5.7 copy-start.14
  439.2 5.7 copy-start.21
  439.2 5.7 copy-start.23
  446.4 24.9 %copy-start.16 = (bf16[32,512]{1,0:T(8,128)(2,1)}, bf16[32,512]{1,0:T(8,128)(2,1)S(1)}, u32[]{:S(2)}) copy-start(bf16[32,512]{1,0:T(8,128)(2,1)S(1)} %get-tuple-element.8) | copy-start | bytes 98308
  468.1 169.2 %reduce-scatter.11.cloned.1.call-start = ((), (), s32[]{:S(2)}) async-start(), calls=%async_computation.16 | async-start | bytes 2162688 | tf_op jit(solution)/shard_map/reduce_scatter | solution.py:113
  471.2 242.9 %all-gather.11.cloned.1.call-start = ((), (), s32[]{:S(2)}) async-start(), calls=%async_computation.13 | async-start | bytes 1081344 | tf_op jit(solution)/shard_map/all_gather | solution.py:75
  545.6 91.7 %copy-start.25 = (bf16[32,32]{1,0:T(8,128)(2,1)}, bf16[32,32]{1,0:T(8,128)(2,1)S(1)}, u32[]{:S(2)}) copy-start(bf16[32,32]{1,0:T(8,128)(2,1)S(1)} %psum.61) | copy-start | bytes 6148
  545.6 255.1 %reduce-scatter.17.cloned.1.call-start = ((), (), s32[]{:S(2)}) async-start(), calls=%async_computation.19 | async-start | bytes 540672 | tf_op jit(solution)/shard_map/reduce_scatter | solution.py:111
  664.9 199.9 %reduce-scatter.15.cloned.1.call-start = ((), (), s32[]{:S(2)}) async-start(), calls=%async_computation.18 | async-start | bytes 2162688 | tf_op jit(solution)/shard_map/reduce_scatter | solution.py:113
  668.0 36.1 %copy-start.29 = (bf16[32,32]{1,0:T(8,128)(2,1)S(1)}, bf16[32,32]{1,0:T(8,128)(2,1)}, u32[]{:S(2)}) copy-start(bf16[32,32]{1,0:T(8,128)(2,1)} %copy-done.28) | copy-start | bytes 6148
  668.0 37.0 %copy-start.9 = (bf16[32,512]{1,0:T(8,128)(2,1)S(1)}, bf16[32,512]{1,0:T(8,128)(2,1)}, u32[]{:S(2)}) copy-start(bf16[32,512]{1,0:T(8,128)(2,1)} %get-tuple-element.13) | copy-start | bytes 98308
  668.0 37.0 %copy-start.26 = (bf16[32,32]{1,0:T(8,128)(2,1)S(1)}, bf16[32,32]{1,0:T(8,128)(2,1)}, u32[]{:S(2)}) copy-start(bf16[32,32]{1,0:T(8,128)(2,1)} %copy-done.25) | copy-start | bytes 6148
  691.0 22.1 %all-to-all-start.3 = ((bf16[32,32,128]{2,1,0:T(8,128)(2,1)}), bf16[32,32,128]{2,1,0:T(8,128)(2,1)}, u32[]{:S(2)}, u32[]{:S(2)}) async-start(bf16[32,32,128]{2,1,0:T(8,128)(2,1)} %stack.15), calls=%async_computation.3 | async-start | bytes 524288 | tf_op jit(solution)/shard_map/all_to_all | solution.py:16
  714.1 5.6 copy-start.38
  719.7 6.3 copy-start.18
  719.7 80.3 %copy-start.7 = (bf16[32,512]{1,0:T(8,128)(2,1)S(1)}, bf16[32,512]{1,0:T(8,128)(2,1)}, u32[]{:S(2)}) copy-start(bf16[32,512]{1,0:T(8,128)(2,1)} %get-tuple-element.11) | copy-start | bytes 98308
  719.7 80.3 %copy-start.20 = (f32[32,512]{1,0:T(8,128)S(1)}, f32[32,512]{1,0:T(8,128)}, u32[]{:S(2)}) copy-start(f32[32,512]{1,0:T(8,128)} %convolution_add_fusion.2) | copy-start | bytes 196612
  723.8 143.5 %copy-start.43 = (s32[128]{0:T(128)S(1)}, s32[128]{0:T(128)}, u32[]{:S(2)}) copy-start(s32[128]{0:T(128)} %fusion.54) | copy-start | bytes 1540
  (11 other events, 15.8 us)
Sparse Core Ops, SparseCore 0:
  10.5 53.6 all-gather.4
  142.5 43.7 all-gather.6
  190.0 81.9 reduce-scatter.8
  275.7 86.3 reduce-scatter.6
  364.4 48.9 all-gather.8
  468.2 79.3 reduce-scatter.12
  551.4 85.8 reduce-scatter.10
  639.7 49.4 all-gather.10
  692.9 82.0 reduce-scatter.16
  778.7 85.9 reduce-scatter.14
